TPU v7x, 128 devices: a whole 4x4x4 slice. The times are simulated.
128 devices in a mesh: blk: 32 (over y, x, core), grp: 4 (over z).
Axes of the slice: x: 4, y: 4, z: 4, core: 2. Of those that a mesh axis runs over, the one named last changes fastest.
Arguments:
- sky_map: bfloat16 [256, 1048576], P(None, ('blk', 'grp')), may hold values from -128 to 128
- fg_templates: bfloat16 [256, 16], replicated, may hold values from -0.375 to 0.375
- cycle_len: int32 [512], P(('blk', 'grp')), may hold values from 512 to 2048, as said below
- beam_profile: float32 [8, 1024], replicated, may hold values from 0.2 to 2
- beam_index: int32 [256], P('blk'), may hold values from 0 to 7
Outputs:
- filtered: float32 [1024, 256, 2, 1024], P(None, 'blk', None, 'grp')
Inputs may be any that keep to these rules, and one draw needn't show every extreme that they name: `cycle_len`: some cycle has exactly 2048 pixels.
All inputs are finite; a program needn't handle non-finite values.
Results may differ from a plain program's by a relative error of at most 0.0064.
Values may be sent and summed in bfloat16 or wider, within the bound.
No kernel may reach another device: no remote copies, remote signals or barrier semaphores. Data moves between devices by JAX's collectives and lax.ppermute only.
A program may use at most 192 MiB of HBM per device.

v0:
```python
import jax
import jax.numpy as jnp
from jax import lax
from jax.sharding import PartitionSpec as P

RPIX = 2048
L = 1024
M_DEV = 256


def cycle_table(length, m_width):
    slots = jnp.arange(RPIX, dtype=jnp.int32)
    orders = jnp.arange(m_width, dtype=jnp.int32)
    phase = orders[None, :] * (2 * slots[:, None] + 1) % (2 * length)
    angle = jnp.pi * phase.astype(jnp.float32) / length.astype(jnp.float32)
    weight = jnp.where(slots < length, 1.0, 0.0).astype(jnp.float32) * lax.rsqrt(
        length.astype(jnp.float32)
    )
    table = jnp.concatenate([jnp.cos(angle), -jnp.sin(angle)], axis=1) * weight[:, None]
    return table.astype(jnp.bfloat16)


def theta_table(cycle_ids, n_cycle):
    degrees = jnp.arange(L, dtype=jnp.int32)
    odd = 2 * cycle_ids + 1
    phase = degrees[:, None] * odd[None, :] % (4 * n_cycle)
    angle = jnp.pi * phase.astype(jnp.float32) / (2.0 * n_cycle)
    weight = jnp.sin(jnp.pi * odd.astype(jnp.float32) / (2.0 * n_cycle)) * (
        2.0 / jnp.sqrt(jnp.float32(n_cycle))
    )
    return (jnp.cos(angle) * weight[None, :]).astype(jnp.bfloat16)


def body(sky_map, fg_templates, cycle_len, beam_profile, beam_index):
    n_blk = lax.axis_size("blk")
    n_grp = lax.axis_size("grp")
    cycle_dev = cycle_len.shape[0]
    n_chan = sky_map.shape[0]
    chan_dev = n_chan // n_blk
    m_width = M_DEV * n_grp
    n_cycle = cycle_dev * n_blk * n_grp
    slots = jnp.arange(RPIX, dtype=jnp.int32)
    valid = (slots[None, :] < cycle_len[:, None]).reshape(-1)
    masked = jnp.where(valid[None, :], sky_map, jnp.zeros((), jnp.bfloat16))
    mode_amps = jnp.dot(fg_templates.T, masked, preferred_element_type=jnp.float32).astype(
        jnp.bfloat16
    )
    gram_part = jnp.dot(mode_amps, mode_amps.T, preferred_element_type=jnp.float32)
    cross_part = lax.dot_general(
        mode_amps, masked, (((1,), (1,)), ((), ())), preferred_element_type=jnp.float32
    )
    amps_wide = mode_amps.astype(jnp.float32)
    gram_sum = lax.psum(gram_part, ("blk", "grp"))
    lower = jnp.linalg.cholesky(gram_sum)
    basis = jax.scipy.linalg.solve_triangular(lower, amps_wide, lower=True)
    proj_part = jax.scipy.linalg.solve_triangular(lower, cross_part, lower=True)
    projected = lax.psum(proj_part, ("blk", "grp"))
    correction = jnp.dot(projected.T, basis, precision=lax.Precision.HIGHEST)
    cleaned = (masked.astype(jnp.float32) - correction).astype(jnp.bfloat16)
    pieces = []
    for local in range(cycle_dev):
        block = cleaned[:, local * RPIX : (local + 1) * RPIX]
        table = cycle_table(cycle_len[local], m_width)
        pieces.append(
            jnp.dot(block, table, preferred_element_type=jnp.float32).astype(jnp.bfloat16)
        )
    fourier = jnp.stack(pieces, 0).reshape(cycle_dev, n_chan, 2, m_width)
    position = jnp.arange(n_cycle, dtype=jnp.int32)
    moved = lax.all_to_all(
        lax.all_to_all(fourier, "blk", split_axis=1, concat_axis=0, tiled=True),
        "grp",
        split_axis=3,
        concat_axis=0,
        tiled=True,
    )
    group_id = position // (n_blk * cycle_dev)
    block_id = position // cycle_dev % n_blk
    cycle_ids = (block_id * n_grp + group_id) * cycle_dev + position % cycle_dev
    moved = moved.reshape(n_cycle, chan_dev * 2 * M_DEV)
    theta_tab = theta_table(cycle_ids, n_cycle)
    harmonic = jnp.dot(theta_tab, moved, preferred_element_type=jnp.float32).reshape(
        L, chan_dev, 2, M_DEV
    )
    onehot = (
        beam_index[:, None] == jnp.arange(beam_profile.shape[0], dtype=jnp.int32)[None, :]
    ).astype(jnp.float32)
    profiles = jnp.dot(onehot, beam_profile, precision=lax.Precision.HIGHEST)
    shaped = harmonic * profiles.T[:, :, None, None]
    orders = lax.axis_index("grp") * M_DEV + jnp.arange(M_DEV, dtype=jnp.int32)
    mweight = 0.25 + orders.astype(jnp.float32) / m_width
    weighted = shaped * mweight[None, None, None, :]
    power_part = jnp.sum(weighted * weighted, axis=(0, 2, 3))
    power = lax.psum(power_part, "grp")
    return weighted * lax.rsqrt(power / (2.0 * L * m_width) + 1e-06)[None, :, None, None]


def solution(mesh):
    return jax.shard_map(
        body,
        mesh=mesh,
        in_specs=(P(None, ("blk", "grp")), P(), P(("blk", "grp")), P(), P("blk")),
        out_specs=P(None, "blk", None, "grp"),
        check_vma=False,
    )
```

profile of v0, /device:TPU:0, one launch (start us, length us, event | category | flops | bytes accessed | tf_op | source)
XLA Modules:
  0.0 859.5 jit_solution(13465190245039165098)
XLA Ops:
  0.0 0.0 copy-start
  0.0 1.4 fusion.120
  6.2 0.7 fusion.87
  7.0 2.9 convolution_convert_fusion
  9.9 0.2 fusion.121
  10.1 3.4 fusion.50
  13.5 68.2 %psum.21 = f32[16,16]{0,1:T(8,128)S(1)} all-reduce(f32[16,16]{0,1:T(8,128)S(1)} %fusion.121), channel_id=1, replica_groups=mesh['blk'=32,'grp'=4] {'blk','grp'}, use_global_device_ids=true, to_apply=%region_0.1 | all-reduce | flops 256 | bytes 2048 | tf_op jit(solution)/shard_map/psum | solution.py:53
  81.7 0.1 copy.38
  81.8 1.5 cholesky.16
  83.3 0.7 compare_reduce_fusion
  84.0 0.7 fusion.88
  84.7 1.2 custom-call.10
  85.9 0.4 fusion.89
  86.3 0.2 fusion.91
  86.5 62.3 %psum.22 = f32[16,256]{1,0:T(8,128)S(1)} all-reduce(f32[16,256]{1,0:T(8,128)S(1)} %fusion.91), channel_id=1, replica_groups=mesh['blk'=32,'grp'=4] {'blk','grp'}, use_global_device_ids=true, to_apply=%region_3.4 | all-reduce | flops 4096 | bytes 32768 | tf_op jit(solution)/shard_map/psum | solution.py:57
  148.9 0.7 select_multiply_fusion.3
  149.6 8.9 %fusion.5 = bf16[256,8192]{1,0:T(8,128)(2,1)S(1)} fusion(f32[16,256]{1,0:T(8,128)S(1)} %psum.22, f32[16,8192]{1,0:T(8,128)S(1)} %fusion.89, bf16[256,8192]{1,0:T(8,128)(2,1)} %param.5, pred[8192]{0:T(1024)(128)(4,1)S(1)} %bitcast.62), kind=kOutput, calls=%fused_computation.16 | convolution fusion | flops 411041792 | bytes 8937472 | tf_op jit(solution)/shard_map/dot_general | solution.py:58
  158.5 0.0 copy-start.1
  158.5 451.2 %fusion.49 = (f32[2048,1024]{1,0:T(8,128)S(1)}, f32[2048,1024]{1,0:T(8,128)}, f32[2048,1024]{1,0:T(8,128)}, f32[2048,1024]{1,0:T(8,128)}, f32[2048,1024]{1,0:T(8...) fusion(f32[]{:T(128)S(6)} %convert_element_type.91, pred[]{:T(512)S(6)} %lt.110, ...), kind=kLoop, calls=%fused_computation.64 | loop fusion | flops 94371840 | bytes 67117088 | tf_op jit(solution)/shard_map/cos | solution.py:19
  609.7 0.0 copy-done.1
  609.7 6.3 fusion.51
  616.0 0.8 stack.15
  616.8 0.6 select_multiply_fusion.2
  617.4 8.5 fusion.54
  626.0 0.8 stack.16
  626.8 0.6 select_multiply_fusion.1
  627.4 9.5 %fusion.57 = bf16[256,2048]{1,0:T(8,128)(2,1)} fusion(f32[2048,1024]{1,0:T(8,128)} %get-tuple-element.7, f32[2048,1024]{1,0:T(8,128)} %get-tuple-element.10, f32[2048]{0:T(1024)S(1)} %select_multiply_fusion.1, bf16[256,8192]{1,0:T(8,128)(2,1)} %copy-done.1), kind=kOutput, calls=%fused_computation.72 | convolution fusion | flops 2160590848 | bytes 18882560 | tf_op jit(solution)/shard_map/dot_general | solution.py:65
  636.9 1.8 stack.17
  638.7 0.6 select_multiply_fusion
  639.3 9.5 %fusion.60 = bf16[256,2048]{1,0:T(8,128)(2,1)} fusion(f32[2048,1024]{1,0:T(8,128)} %get-tuple-element.8, f32[2048,1024]{1,0:T(8,128)} %get-tuple-element.9, f32[2048]{0:T(1024)S(1)} %select_multiply_fusion, bf16[256,8192]{1,0:T(8,128)(2,1)} %copy-done.1), kind=kOutput, calls=%fused_computation.73 | convolution fusion | flops 2160590848 | bytes 18882560 | tf_op jit(solution)/shard_map/dot_general | solution.py:65
  648.8 2.6 stack.18
  651.4 7.6 pad_maximum_fusion
  659.0 55.9 %all_to_all.33 = bf16[4,256,2,1024]{3,2,0,1:T(2,128)(2,1)S(1)} all-to-all(bf16[4,256,2,1024]{3,2,0,1:T(2,128)(2,1)S(1)} %pad_maximum_fusion), channel_id=1, replica_groups=mesh['blk'=32,'grp'=4] {'blk'}, dimensions={1} | all-to-all | bytes 8388608 | tf_op jit(solution)/shard_map/all_to_all | solution.py:70
  714.9 2.3 copy.55
  717.3 2.5 copy.44
  719.7 7.3 copy.45
  727.0 4.9 all-to-all-start.1
  731.9 0.1 sine_multiply_fusion
  732.0 0.0 copy-done
  732.0 0.2 convolution_bitcast_fusion
  732.2 49.1 %all-to-all-done.1 = bf16[128,8,2,1024]{0,1,2,3:T(8,128)(2,1)} async-done(((bf16[128,8,2,1024]{0,1,2,3:T(8,128)(2,1)}), bf16[128,8,2,1024]{0,1,2,3:T(8,128)(2,1)}, u32[]{:S(2)}, u32[]{:S(2)}) %all-to-all-start.1) | async-done | bytes 4194336 | tf_op jit(solution)/shard_map/all_to_all | solution.py:69
  781.3 9.0 %copy.47 = bf16[4,128,8,2,256]{4,3,2,1,0:T(2,128)(2,1)} copy(bf16[4,128,8,2,256]{1,2,3,4,0:T(8,128)(2,1)} %bitcast.18) | data formatting | bytes 8388608 | tf_op jit(solution)/shard_map/all_to_all | solution.py:69
  790.3 7.8 reshape.135
  798.1 6.5 copy.48
  804.6 17.2 %multiply_reduce_fusion = (f32[8]{0:T(128)S(1)}, f32[1024,8,2,256]{3,0,2,1:T(8,128)}) fusion(f32[256]{0:T(256)S(1)} %multiply_add_fusion.1, f32[1024,8]{0,1:T(8,128)S(1)} %convolution_bitcast_fusion, bf16[8,2,256,512]{3,2,1,0:T(8,128)(2,1)} %bitcast.55, f32[512]{0:T(512)S(1)} %sine_multiply_fusion, s32[512]{0:T(512)S(1)} %fusion.104), kind=kOutput, calls=%fused_computation.8 | convolution fusion | flops 4320133120 | bytes 21009440 | tf_op jit(solution)/shard_map/dot_general | solution.py:81
  821.9 8.8 %psum.23 = f32[8]{0:T(128)S(1)} all-reduce(f32[8]{0:T(128)S(1)} %get-tuple-element.17), channel_id=1, replica_groups=mesh['blk'=32,'grp'=4] {'grp'}, use_global_device_ids=true, to_apply=%region_5.6 | all-reduce | flops 8 | bytes 64 | tf_op jit(solution)/shard_map/psum | solution.py:93
  830.7 7.0 fusion.4
  837.8 21.5 %copy.49 = f32[1024,8,2,256]{3,2,1,0:T(2,128)} copy(f32[1024,8,2,256]{3,0,2,1:T(8,128)S(1)} %fusion.4) | data formatting | bytes 33554432 | tf_op jit(solution)/shard_map/mul | solution.py:94
  (9 shorter events, 0.1 us)
Async XLA Ops:
  0.0 732.0 %copy-start = (f32[8,1024]{1,0:T(8,128)S(1)}, f32[8,1024]{1,0:T(8,128)}, u32[]{:S(2)}) copy-start(f32[8,1024]{1,0:T(8,128)} %param.8) | copy-start | bytes 98308
  158.5 451.2 %copy-start.1 = (bf16[256,8192]{1,0:T(8,128)(2,1)}, bf16[256,8192]{1,0:T(8,128)(2,1)S(1)}, u32[]{:S(2)}) copy-start(bf16[256,8192]{1,0:T(8,128)(2,1)S(1)} %fusion.5) | copy-start | bytes 12582916
  719.7 12.3 %copy-start.2 = (s32[8]{0:T(128)S(1)}, s32[8]{0:T(128)}, u32[]{:S(2)}) copy-start(s32[8]{0:T(128)} %param.9) | copy-start | bytes 100
  727.0 54.3 %all-to-all-start.1 = ((bf16[128,8,2,1024]{0,1,2,3:T(8,128)(2,1)}), bf16[128,8,2,1024]{0,1,2,3:T(8,128)(2,1)}, u32[]{:S(2)}, u32[]{:S(2)}) async-start(bf16[128,8,2,1024]{0,1,2,3:T(8,128)(2,1)} %copy.45), calls=%async_computation.1 | async-start | bytes 8388608 | tf_op jit(solution)/shard_map/all_to_all | solution.py:69
where the time goes:
time: 867 us; the launch traced here: 859 us
  other arithmetic  473 us (55%)
  blocking collectives  195 us (22%)
  matrix products  67.2 us (8%)
  local copies, waits for them, and re-layouts  64.4 us (7%)
  waiting for transfers between devices  49.1 us (6%)
    cos x1, other arithmetic, cycle_table(): jnp.cos(angle)  451 us
    psum x1, blocking collectives, body(): gram_sum = lax.psum(gram_part, ('blk', 'grp'))  68.2 us
    psum x1, blocking collectives, body(): projected = lax.psum(proj_part, ('blk', 'grp'))  62.3 us
    all_to_all x1, blocking collectives, body(): lax.all_to_all(fourier, 'blk', split_axis=1, concat_axis=0, tiled=True)  55.9 us
    all_to_all x1, waiting for transfers between devices, body(): lax.all_to_all(lax.all_to_all(fourier, 'blk', split_axis=1, concat_axis=0...  49.1 us
    dot_general x4, matrix products, body(): jnp.dot(block, table, preferred_element_type=jnp.float32)  33.9 us
    mul x1, local copies, waits for them, and re-layouts, body(): weighted * lax.rsqrt(power / (2.0 * L * m_width) + 1e-06)[None, :, None,...  21.5 us
  transfers between devices with their start and end apart: 1, of which 1 were waited for; matrix products, arithmetic and copies ran while one was open for 0% of the time, Pallas kernels for 0%

commit v1 on v0

--- a/solution.py
+++ b/solution.py
@@ -66,12 +66,20 @@
         )
     fourier = jnp.stack(pieces, 0).reshape(cycle_dev, n_chan, 2, m_width)
     position = jnp.arange(n_cycle, dtype=jnp.int32)
-    moved = lax.all_to_all(
-        lax.all_to_all(fourier, "blk", split_axis=1, concat_axis=0, tiled=True),
-        "grp",
-        split_axis=3,
-        concat_axis=0,
-        tiled=True,
+    moved = jnp.concatenate(
+        lax.all_to_all(
+            jnp.stack(
+                jnp.split(
+                    lax.all_to_all(fourier, "blk", split_axis=1, concat_axis=0, tiled=True),
+                    lax.axis_size("grp"),
+                    axis=3,
+                )
+            ),
+            "grp",
+            0,
+            0,
+        ),
+        axis=0,
     )
     group_id = position // (n_blk * cycle_dev)
     block_id = position // cycle_dev % n_blk

time: 867 us -> 860 us (level)
  local copies, waits for them, and re-layouts: 64.4 us -> 55.1 us
    all_to_all x3 -> x2, local copies, waits for them, and re-layouts: 12.1 us -> 2.96 us  [body(): lax.all_to_all(fourier, 'blk', split_axis=1, concat_axis=0, tiled=True)]
where the time goes in v1:
time: 860 us; the launch traced here: 853 us
  other arithmetic  475 us (55%)
  blocking collectives  195 us (23%)
  matrix products  67.2 us (8%)
  local copies, waits for them, and re-layouts  55.1 us (6%)
  waiting for transfers between devices  49.1 us (6%)
    cos x1, other arithmetic, cycle_table(): jnp.cos(angle)  451 us
    psum x1, blocking collectives, body(): gram_sum = lax.psum(gram_part, ('blk', 'grp'))  68.2 us
    psum x1, blocking collectives, body(): projected = lax.psum(proj_part, ('blk', 'grp'))  62.3 us
    all_to_all x1, blocking collectives, body(): lax.all_to_all(fourier, 'blk', split_axis=1, concat_axis=0, tiled=True)  55.7 us
    all_to_all x1, waiting for transfers between devices, body(): lax.all_to_all(jnp.stack(jnp.split(lax.all_to_all(fourier, 'blk', split_a...  49.1 us
    dot_general x4, matrix products, body(): jnp.dot(block, table, preferred_element_type=jnp.float32)  33.9 us
    mul x1, local copies, waits for them, and re-layouts, body(): weighted * lax.rsqrt(power / (2.0 * L * m_width) + 1e-06)[None, :, None,...  21.5 us
    dot_general x1, matrix products, body(): jnp.dot(theta_tab, moved, preferred_element_type=jnp.float32)  17.2 us
  transfers between devices with their start and end apart: 1, of which 1 were waited for; matrix products, arithmetic and copies ran while one was open for 0% of the time, Pallas kernels for 0%

profile of v1, /device:TPU:0, one launch (start us, length us, event | category | flops | bytes accessed | tf_op | source)
XLA Modules:
  0.0 852.5 jit_solution(15851574456957401119)
XLA Ops:
  0.0 0.0 copy-start
  0.0 1.4 fusion.120
  6.2 0.7 fusion.87
  7.0 2.9 convolution_convert_fusion
  9.9 0.2 fusion.121
  10.1 3.4 fusion.50
  13.5 68.2 %psum.21 = f32[16,16]{0,1:T(8,128)S(1)} all-reduce(f32[16,16]{0,1:T(8,128)S(1)} %fusion.121), channel_id=1, replica_groups=mesh['blk'=32,'grp'=4] {'blk','grp'}, use_global_device_ids=true, to_apply=%region_0.1 | all-reduce | flops 256 | bytes 2048 | tf_op jit(solution)/shard_map/psum | solution.py:53
  81.7 0.1 copy.26
  81.8 1.5 cholesky.16
  83.3 0.7 compare_reduce_fusion
  84.0 0.7 fusion.88
  84.7 1.2 custom-call.10
  85.9 0.4 fusion.89
  86.4 0.2 fusion.91
  86.6 62.3 %psum.22 = f32[16,256]{1,0:T(8,128)S(1)} all-reduce(f32[16,256]{1,0:T(8,128)S(1)} %fusion.91), channel_id=1, replica_groups=mesh['blk'=32,'grp'=4] {'blk','grp'}, use_global_device_ids=true, to_apply=%region_3.4 | all-reduce | flops 4096 | bytes 32768 | tf_op jit(solution)/shard_map/psum | solution.py:57
  148.9 0.7 select_multiply_fusion.3
  149.7 8.9 %fusion.5 = bf16[256,8192]{1,0:T(8,128)(2,1)S(1)} fusion(f32[16,256]{1,0:T(8,128)S(1)} %psum.22, f32[16,8192]{1,0:T(8,128)S(1)} %fusion.89, bf16[256,8192]{1,0:T(8,128)(2,1)} %param.5, pred[8192]{0:T(1024)(128)(4,1)S(1)} %bitcast.67), kind=kOutput, calls=%fused_computation.16 | convolution fusion | flops 411041792 | bytes 8937472 | tf_op jit(solution)/shard_map/dot_general | solution.py:58
  158.5 451.2 %fusion.49 = (f32[2048,1024]{1,0:T(8,128)S(1)}, f32[2048,1024]{1,0:T(8,128)}, f32[2048,1024]{1,0:T(8,128)}, f32[2048,1024]{1,0:T(8,128)}, f32[2048,1024]{1,0:T(8...) fusion(f32[]{:T(128)S(6)} %convert_element_type.91, pred[]{:T(512)S(6)} %lt.110, ...), kind=kLoop, calls=%fused_computation.65 | loop fusion | flops 94371840 | bytes 67117088 | tf_op jit(solution)/shard_map/cos | solution.py:19
  609.7 0.0 copy-done.1
  609.7 6.3 fusion.51
  616.1 0.8 stack.30
  616.9 0.6 select_multiply_fusion.2
  617.4 8.5 fusion.54
  626.0 0.8 stack.31
  626.8 0.6 select_multiply_fusion.1
  627.4 9.5 %fusion.57 = bf16[256,2048]{1,0:T(8,128)(2,1)} fusion(f32[2048,1024]{1,0:T(8,128)} %get-tuple-element.11, f32[2048,1024]{1,0:T(8,128)} %get-tuple-element.14, f32[2048]{0:T(1024)S(1)} %select_multiply_fusion.1, bf16[256,8192]{1,0:T(8,128)(2,1)} %copy-done.1), kind=kOutput, calls=%fused_computation.73 | convolution fusion | flops 2160590848 | bytes 18882560 | tf_op jit(solution)/shard_map/dot_general | solution.py:65
  636.9 1.8 stack.32
  638.7 0.6 select_multiply_fusion
  639.3 9.5 %fusion.60 = bf16[256,2048]{1,0:T(8,128)(2,1)} fusion(f32[2048,1024]{1,0:T(8,128)} %get-tuple-element.12, f32[2048,1024]{1,0:T(8,128)} %get-tuple-element.13, f32[2048]{0:T(1024)S(1)} %select_multiply_fusion, bf16[256,8192]{1,0:T(8,128)(2,1)} %copy-done.1), kind=kOutput, calls=%fused_computation.74 | convolution fusion | flops 2160590848 | bytes 18882560 | tf_op jit(solution)/shard_map/dot_general | solution.py:65
  648.8 2.6 stack.33
  651.5 7.6 pad_maximum_fusion
  659.1 55.7 %all_to_all.23 = bf16[4,256,2,1024]{3,2,0,1:T(2,128)(2,1)S(1)} all-to-all(bf16[4,256,2,1024]{3,2,0,1:T(2,128)(2,1)S(1)} %pad_maximum_fusion), channel_id=1, replica_groups=mesh['blk'=32,'grp'=4] {'blk'}, dimensions={1} | all-to-all | bytes 8388608 | tf_op jit(solution)/shard_map/all_to_all | solution.py:73
  714.7 2.3 copy.40
  717.1 0.6 copy.32
  717.7 0.3 slice_bitcast_fusion.3
  718.1 0.0 copy-start.2
  718.1 2.3 pad_maximum_fusion.1
  720.4 5.1 all-to-all-start.1
  725.5 0.1 sine_multiply_fusion
  725.5 0.2 convolution_bitcast_fusion
  725.7 49.1 %all-to-all-done.1 = bf16[4,128,8,2,256]{4,2,3,1,0:T(8,128)(2,1)} async-done(((bf16[4,128,8,2,256]{4,2,3,1,0:T(8,128)(2,1)}), bf16[4,128,8,2,256]{4,2,3,1,0:T(8,128)(2,1)}, u32[]{:S(2)}, u32[]{:S(2)}) %all-to-all-start.1) | async-done | bytes 4194336 | tf_op jit(solution)/shard_map/all_to_all | solution.py:70
  774.8 8.5 copy.33
  783.4 7.8 reshape_reshape.3
  791.1 6.5 copy.34
  797.7 17.2 %multiply_reduce_fusion = (f32[8]{0:T(128)S(1)}, f32[1024,8,2,256]{3,0,2,1:T(8,128)}) fusion(f32[256]{0:T(256)S(1)} %multiply_add_fusion.1, f32[1024,8]{0,1:T(8,128)S(1)} %convolution_bitcast_fusion, bf16[8,2,256,512]{3,2,1,0:T(8,128)(2,1)} %bitcast.60, f32[512]{0:T(512)S(1)} %sine_multiply_fusion, s32[512]{0:T(512)S(1)} %fusion.104), kind=kOutput, calls=%fused_computation.8 | convolution fusion | flops 4320133120 | bytes 21009440 | tf_op jit(solution)/shard_map/dot_general | solution.py:89
  814.9 8.9 %psum.23 = f32[8]{0:T(128)S(1)} all-reduce(f32[8]{0:T(128)S(1)} %get-tuple-element.21), channel_id=1, replica_groups=mesh['blk'=32,'grp'=4] {'grp'}, use_global_device_ids=true, to_apply=%region_5.6 | all-reduce | flops 8 | bytes 64 | tf_op jit(solution)/shard_map/psum | solution.py:101
  823.8 7.0 fusion.4
  830.8 21.5 %copy.35 = f32[1024,8,2,256]{3,2,1,0:T(2,128)} copy(f32[1024,8,2,256]{3,0,2,1:T(8,128)S(1)} %fusion.4) | data formatting | bytes 33554432 | tf_op jit(solution)/shard_map/mul | solution.py:102
  (10 shorter events, 0.1 us)
Async XLA Ops:
  0.0 725.5 %copy-start = (f32[8,1024]{1,0:T(8,128)S(1)}, f32[8,1024]{1,0:T(8,128)}, u32[]{:S(2)}) copy-start(f32[8,1024]{1,0:T(8,128)} %param.8) | copy-start | bytes 98308
  158.5 451.2 %copy-start.1 = (bf16[256,8192]{1,0:T(8,128)(2,1)}, bf16[256,8192]{1,0:T(8,128)(2,1)S(1)}, u32[]{:S(2)}) copy-start(bf16[256,8192]{1,0:T(8,128)(2,1)S(1)} %fusion.5) | copy-start | bytes 12582916
  718.1 7.5 copy-start.2
  720.4 54.5 %all-to-all-start.1 = ((bf16[4,128,8,2,256]{4,2,3,1,0:T(8,128)(2,1)}), bf16[4,128,8,2,256]{4,2,3,1,0:T(8,128)(2,1)}, u32[]{:S(2)}, u32[]{:S(2)}) async-start(bf16[4,128,8,2,256]{4,2,3,1,0:T(8,128)(2,1)} %pad_maximum_fusion.1), calls=%async_computation.1 | async-start | bytes 8388608 | tf_op jit(solution)/shard_map/all_to_all | solution.py:70
